TPU v7x, 32 devices: a whole 2x2x4 slice. The times are simulated.
32 devices in a mesh: seq: 4 (over y, x), batch: 8 (over z, core).
Axes of the slice: x: 2, y: 2, z: 4, core: 2. Of those that a mesh axis runs over, the one named last changes fastest.
Arguments:
- feats: bfloat16 [768, 4096], P('seq', 'batch'), parts along dimension 1, may hold values from -6 to 6
- qkv_weight: bfloat16 [768, 2304], replicated, may hold values from -0.21875 to 0.21875
- beta_weight: bfloat16 [768, 6], replicated, may hold values from -0.21875 to 0.21875
- beta_bias: float32 [6], replicated, may hold values from -7 to 0.5
- out_gain: float32 [768], replicated, may hold values from 0.1 to 1.9
Outputs:
- mixed: bfloat16 [4096, 768], P(('batch', 'seq')), parts along dimension 0
There are 8 independent parts, one for each index of `batch`. A program takes and returns all parts, laid end to end along the dimension named above; an argument that names none is the same for every part. Nothing has to cross between parts.
All inputs are finite; a program needn't handle non-finite values.
Results may differ from a plain program's by a relative error of at most 0.012.
Values may be sent and summed in bfloat16 or wider, within the bound.
No kernel may reach another device: no remote copies, remote signals or barrier semaphores. Data moves between devices by JAX's collectives and lax.ppermute only.
A program may use at most 64 MiB of HBM per device.

v0:
```python
import jax
import jax.numpy as jnp
from jax import lax
from jax.sharding import PartitionSpec as P

HEADS = 6
HD = 128
GROUP = 64
HIGHEST_ACCURACY = lax.Precision.HIGHEST


def entering(value, axis, join, neutral):
    count, mine = (lax.axis_size(axis), lax.axis_index(axis))
    pieces = jax.tree.map(lambda part: lax.all_gather(part, axis), value)
    running = jax.tree.map(
        lambda part, zero: jnp.full_like(part, 0) + jnp.asarray(zero, part.dtype), value, neutral
    )

    def turn(position, running):
        longer = join(running, jax.tree.map(lambda part: part[position], pieces))
        return jax.tree.map(lambda new, old: jnp.where(position < mine, new, old), longer, running)

    return lax.fori_loop(0, count - 1, turn, running)


def unit_inverse(gram):
    eye_block = jnp.eye(gram.shape[-1], dtype=jnp.float32)
    negated = -jnp.tril(gram, -1)
    inverse = eye_block + negated
    power = negated
    for level in range(5):
        power = jnp.einsum("nhij,nhjk->nhik", power, power, precision=HIGHEST_ACCURACY)
        inverse = inverse + jnp.einsum(
            "nhij,nhjk->nhik", inverse, power, precision=HIGHEST_ACCURACY
        )
    return inverse


def prepare(qkv, beta):
    rows = qkv.shape[0]
    blocks_count = rows // GROUP
    pieces = qkv.astype(jnp.float32).reshape(rows, 3, HEADS, HD)
    query = pieces[:, 0]
    keys = pieces[:, 1]
    values = pieces[:, 2]
    query = query * lax.rsqrt(jnp.sum(query * query, -1, keepdims=True) + 1e-06)
    keys = keys * lax.rsqrt(jnp.sum(keys * keys, -1, keepdims=True) + 1e-06)

    def blocks(arr):
        return arr.reshape(blocks_count, GROUP, HEADS, arr.shape[-1]).transpose(0, 2, 1, 3)

    query = blocks(query)
    keys = blocks(keys)
    values = blocks(values)
    rates = blocks(beta[:, :, None])
    weighted = keys * rates
    gram = jnp.einsum("nhik,nhjk->nhij", weighted, keys, precision=HIGHEST_ACCURACY)
    inverse = unit_inverse(gram)
    right = jnp.concatenate([weighted, values * rates], -1)
    solved = jnp.einsum("nhij,nhjk->nhik", inverse, right, precision=HIGHEST_ACCURACY)
    wfac = solved[..., :HD]
    ufac = solved[..., HD:]
    scores = jnp.tril(jnp.einsum("nhik,nhjk->nhij", query, keys, precision=HIGHEST_ACCURACY))
    return (query, keys, wfac, ufac, scores)


def finish(outputs, out_gain):
    rows = outputs.shape[0] * GROUP
    flat = outputs.transpose(0, 2, 1, 3).reshape(rows, HEADS, HD)
    power = jnp.mean(flat * flat, -1, keepdims=True) + 1e-06
    normed = flat * lax.rsqrt(power) * out_gain.reshape(HEADS, HD)
    return normed.reshape(rows, HEADS * HD).astype(jnp.bfloat16)


def compose(early, late):
    first_move, first_offset = early
    second_move, second_offset = late
    move = jnp.einsum("hij,hjk->hik", second_move, first_move, precision=HIGHEST_ACCURACY)
    offset = (
        jnp.einsum("hij,hjk->hik", second_move, first_offset, precision=HIGHEST_ACCURACY)
        + second_offset
    )
    return (move, offset)


def body(feats, qkv_weight, beta_weight, beta_bias, out_gain):
    local = lax.all_to_all(feats, "seq", split_axis=1, concat_axis=0, tiled=True)
    qkv = lax.dot_general(
        local, qkv_weight, (((0,), (0,)), ((), ())), preferred_element_type=jnp.float32
    ).astype(jnp.bfloat16)
    logits = lax.dot_general(
        local, beta_weight, (((0,), (0,)), ((), ())), preferred_element_type=jnp.float32
    )
    beta = jax.nn.sigmoid(logits + beta_bias)
    query, keys, wfac, ufac, scores = prepare(qkv, beta)
    eye_heads = jnp.broadcast_to(jnp.eye(HD, dtype=jnp.float32), (HEADS, HD, HD))
    empty = jnp.zeros((HEADS, HD, HD), jnp.float32)

    def first_pass(joint_matrix, item):
        query_block, key_block, weight_block, update_block, state_block = item
        held_value = jnp.einsum(
            "rnf,rfw->rnw", weight_block, joint_matrix, precision=HIGHEST_ACCURACY
        )
        carried_state = joint_matrix[..., HD:]
        residual_value = update_block - held_value[..., HD:]
        output_rows = jnp.einsum(
            "rnf,rfw->rnw", query_block, carried_state, precision=HIGHEST_ACCURACY
        ) + jnp.einsum("fco,fop->fcp", state_block, residual_value, precision=HIGHEST_ACCURACY)
        target_value = jnp.concatenate([-held_value[..., :HD], residual_value], -1)
        joint_matrix = joint_matrix + jnp.einsum(
            "mjr,mjz->mrz", key_block, target_value, precision=HIGHEST_ACCURACY
        )
        return (joint_matrix, output_rows)

    joint_start = jnp.concatenate([eye_heads, empty], -1)
    joint_matrix, local_out = lax.scan(first_pass, joint_start, (query, keys, wfac, ufac, scores))
    moves = joint_matrix[..., :HD]
    offsets = joint_matrix[..., HD:]
    prior = entering((moves, offsets), "seq", compose, (eye_heads, empty))
    incoming = prior[1]

    def second_pass(loop_carry, item):
        query_block, key_block, weight_block, state_block = item
        held_value = jnp.einsum(
            "rnf,rfw->rnw", weight_block, loop_carry, precision=HIGHEST_ACCURACY
        )
        output_rows = jnp.einsum(
            "rnf,rfw->rnw", query_block, loop_carry, precision=HIGHEST_ACCURACY
        ) - jnp.einsum("fco,fop->fcp", state_block, held_value, precision=HIGHEST_ACCURACY)
        loop_carry = loop_carry - jnp.einsum(
            "mjr,mjz->mrz", key_block, held_value, precision=HIGHEST_ACCURACY
        )
        return (loop_carry, output_rows)

    final_carry, added_out = lax.scan(second_pass, incoming, (query, keys, wfac, scores))
    return finish(local_out + added_out, out_gain)


def solution(mesh):
    placed = (P("seq", "batch"), P(), P(), P(), P())
    return jax.shard_map(
        body, mesh=mesh, in_specs=placed, out_specs=P(("batch", "seq"), None), check_vma=False
    )
```

profile of v0, /device:TPU:0, one launch (start us, length us, event | category | flops | bytes accessed | tf_op | source)
XLA Modules:
  0.0 174.5 jit_solution(12034097138395976783)
XLA Ops:
  8.3 5.2 %all-to-all-start = ((bf16[192,4,128]{2,0,1:T(8,128)(2,1)}), bf16[192,4,128]{2,0,1:T(8,128)(2,1)}, u32[]{:S(2)}, u32[]{:S(2)}) async-start(bf16[192,4,128]{2,0,1:T(8,128)(2,1)} %copy_bitcast_fusion), calls=%async_computation | async-start | bytes 393216 | tf_op jit(solution)/shard_map/all_to_all | solution.py:87
  18.8 2.6 %fusion.45 = f32[128,2304]{1,0:T(8,128)} fusion(bf16[768,128]{1,0:T(8,128)(2,1)} %bitcast.12, bf16[768,2304]{1,0:T(8,128)(2,1)S(1)} %copy-done), kind=kOutput, calls=%fused_computation.53 | convolution fusion | flops 453574656 | bytes 4915200 | tf_op jit(solution)/shard_map/dot_general | solution.py:88
  21.4 2.7 %copy.50 = f32[128,2304]{0,1:T(8,128)} copy(f32[128,2304]{1,0:T(8,128)} %fusion.45) | data formatting | bytes 2359296 | tf_op jit(solution)/shard_map/reshape | solution.py:42
  24.1 2.3 %multiply_reduce_fusion.1 = (f32[128,6]{0,1:T(8,128)S(1)}, f32[128,6]{0,1:T(8,128)S(1)}, f32[128,1,6,128]{0,3,2,1:T(8,128)}, f32[128,1,6,128]{0,3,2,1:T(8,128)}, f32[128,1,6,128]{0,3,2,1:T(8,128)}) fusion(f32[128,3,6,128]{0,3,2,1:T(8,128)} %bitcast.151), kind=kLoop, calls=%fused_computation.80 | loop fusion | flops 391680 | bytes 2365440 | tf_op jit(solution)/shard_map/reduce_sum | solution.py:46
  28.3 1.9 %copy.51 = f32[128,1,6,128]{3,0,2,1:T(8,128)} copy(f32[128,1,6,128]{0,3,2,1:T(8,128)} %get-tuple-element.311) | data formatting | bytes 786432 | tf_op jit(solution)/shard_map/slice | solution.py:44
  30.2 1.9 %copy.55 = f32[128,1,6,128]{3,0,2,1:T(8,128)} copy(f32[128,1,6,128]{0,3,2,1:T(8,128)} %get-tuple-element.310) | data formatting | bytes 786432 | tf_op jit(solution)/shard_map/slice | solution.py:45
  46.0 1.9 %copy.57 = f32[128,1,6,128]{3,0,2,1:T(8,128)} copy(f32[128,1,6,128]{0,3,2,1:T(8,128)} %get-tuple-element.309) | data formatting | bytes 786432 | tf_op jit(solution)/shard_map/slice | solution.py:43
  52.3 16.6 %while.38 = (s32[]{:T(128)}, f32[6,128,256]{2,1,0:T(8,128)}, f32[2,6,64,128]{3,2,1,0:T(8,128)}, f32[2,6,64,128]{3,2,1,0:T(8,128)}, f32[2,6,64,128]{3,2,1,0:T(8,1...) while((s32[]{:T(128)}, f32[6,128,256]{2,1,0:T(8,128)}, ...), condition=%wide.region_3.4_spmd, body=%wide.region_2.3_spmd.sunk | while | flops 415678464 | bytes 10029241 | solution.py:116
  52.3 1.9 %fusion.138 = f32[6,64,256]{2,1,0:T(8,128)S(1)} fusion(f32[6,128,256]{2,1,0:T(8,128)} %get-tuple-element.456, f32[2,6,64,128]{3,2,1,0:T(8,128)} %get-tuple-element.468, s32[]{:T(128)} %get-tuple-element.455), kind=kOutput, calls=%fused_computation.13.clone.1 | convolution fusion | flops 150994944 | bytes 1376768 | tf_op jit(solution)/shard_map/while/body/eval_jaxpr/rnf,rfw->rnw/dot_general | solution.py:101
  56.7 2.9 %convolution_add_fusion.10 = f32[6,128,256]{2,1,0:T(8,128)} fusion(f32[6,128,256]{2,1,0:T(8,128)} %get-tuple-element.456, f32[6,64,128]{2,1,0:T(8,128)S(1)} %get-tuple-element.432, f32[6,64,128]{2,1,0:T(8,128)S(1)} %get-tuple-element.433, f32[2,6,64,128]{3,2,1,0:T(8,128)S(1)} %copy-done.3, s32[]{:T(128)} %get-tuple-element.455), kind=kOutput, calls=%fused_computation.clone.1 | convolution fusion | flops 151289856 | bytes 2162692 | tf_op jit(solution)/shard_map/while/body/eval_jaxpr/mjr,mjz->mrz/dot_general | solution.py:110
  60.6 1.9 %fusion.138 = f32[6,64,256]{2,1,0:T(8,128)S(1)} fusion(f32[6,128,256]{2,1,0:T(8,128)} %get-tuple-element.456, f32[2,6,64,128]{3,2,1,0:T(8,128)} %get-tuple-element.468, s32[]{:T(128)} %get-tuple-element.455), kind=kOutput, calls=%fused_computation.13.clone.1 | convolution fusion | flops 150994944 | bytes 1376768 | tf_op jit(solution)/shard_map/while/body/eval_jaxpr/rnf,rfw->rnw/dot_general | solution.py:101
  65.0 2.9 %convolution_add_fusion.10 = f32[6,128,256]{2,1,0:T(8,128)} fusion(f32[6,128,256]{2,1,0:T(8,128)} %get-tuple-element.456, f32[6,64,128]{2,1,0:T(8,128)S(1)} %get-tuple-element.432, f32[6,64,128]{2,1,0:T(8,128)S(1)} %get-tuple-element.433, f32[2,6,64,128]{3,2,1,0:T(8,128)S(1)} %copy-done.3, s32[]{:T(128)} %get-tuple-element.455), kind=kOutput, calls=%fused_computation.clone.1 | convolution fusion | flops 151289856 | bytes 2162692 | tf_op jit(solution)/shard_map/while/body/eval_jaxpr/mjr,mjz->mrz/dot_general | solution.py:110
  68.9 2.1 %fusion.65 = (f32[6,128,128]{2,1,0:T(8,128)}, f32[6,128,128]{2,1,0:T(8,128)}) fusion(f32[6,128,256]{2,1,0:T(8,128)} %get-tuple-element.180), kind=kLoop, calls=%fused_computation.98 | loop fusion | bytes 1572864 | tf_op jit(solution)/shard_map/slice | solution.py:118
  71.8 30.7 %all-gather.5.cloned.1.call-done = f32[24,128,128]{2,1,0:T(8,128)} async-done(((f32[6,128,128]{2,1,0:T(8,128)}), f32[24,128,128]{2,1,0:T(8,128)}) %all-gather.5.cloned.1.call-update) | async-done | bytes 1572880 | tf_op jit(solution)/shard_map/all_gather | solution.py:14
  102.4 32.7 %all-gather.7.cloned.1.call-done = f32[24,128,128]{2,1,0:T(8,128)} async-done(((f32[6,128,128]{2,1,0:T(8,128)}), f32[24,128,128]{2,1,0:T(8,128)}) %all-gather.7.cloned.1.call-update) | async-done | bytes 1572880 | tf_op jit(solution)/shard_map/all_gather | solution.py:14
  135.1 10.2 %while.40 = (s32[]{:T(128)}, f32[6,128,128]{2,1,0:T(8,128)}, s32[]{:T(128)}, f32[4,6,128,128]{3,2,1,0:T(8,128)}, f32[4,6,128,128]{3,2,1,0:T(8,128)}, /*index=5*/s32[]{:T(128)}, s32[]{:T(128)}) while((s32[]{:T(128)}, f32[6,128,128]{2,1,0:T(8,128)}, s32[]{:T(128)}, f32[4,6,128,128]{3,2,1,0:T(8,128)}, f32[4,6,128,128]{3,2,1,0:T(8,128)}, ...), condition=%wide.region_5.6_spmd.clone, body=%wide.region_4.5_spmd.clone.sunk | while | flops 151388160 | bytes 2755167 | solution.py:23
  136.1 2.4 %fusion.154 = f32[6,128,128]{2,1,0:T(8,128)} fusion(f32[6,128,128]{2,1,0:T(8,128)S(1)} %copy.105, f32[4,6,128,128]{3,2,1,0:T(8,128)} %get-tuple-element.491, s32[]{:T(128)} %get-tuple-element.480, f32[4,6,128,128]{3,2,1,0:T(8,128)} %get-tuple-element.490, pred[]{:T(512)S(6)} %compare.4, pred[]{:T(512)S(6)} %lt.30), kind=kOutput, calls=%fused_computation.44.clone.1 | convolution fusion | flops 151388160 | bytes 1968640 | tf_op jit(solution)/shard_map/while/body/eval_jaxpr/hij,hjk->hik/dot_general | solution.py:80
  139.5 2.4 %fusion.154 = f32[6,128,128]{2,1,0:T(8,128)} fusion(f32[6,128,128]{2,1,0:T(8,128)S(1)} %copy.105, f32[4,6,128,128]{3,2,1,0:T(8,128)} %get-tuple-element.491, s32[]{:T(128)} %get-tuple-element.480, f32[4,6,128,128]{3,2,1,0:T(8,128)} %get-tuple-element.490, pred[]{:T(512)S(6)} %compare.4, pred[]{:T(512)S(6)} %lt.30), kind=kOutput, calls=%fused_computation.44.clone.1 | convolution fusion | flops 151388160 | bytes 1968640 | tf_op jit(solution)/shard_map/while/body/eval_jaxpr/hij,hjk->hik/dot_general | solution.py:80
  142.9 2.4 %fusion.154 = f32[6,128,128]{2,1,0:T(8,128)} fusion(f32[6,128,128]{2,1,0:T(8,128)S(1)} %copy.105, f32[4,6,128,128]{3,2,1,0:T(8,128)} %get-tuple-element.491, s32[]{:T(128)} %get-tuple-element.480, f32[4,6,128,128]{3,2,1,0:T(8,128)} %get-tuple-element.490, pred[]{:T(512)S(6)} %compare.4, pred[]{:T(512)S(6)} %lt.30), kind=kOutput, calls=%fused_computation.44.clone.1 | convolution fusion | flops 151388160 | bytes 1968640 | tf_op jit(solution)/shard_map/while/body/eval_jaxpr/hij,hjk->hik/dot_general | solution.py:80
  146.1 13.8 %while.39 = (s32[]{:T(128)}, f32[6,128,128]{2,1,0:T(8,128)}, f32[2,6,64,128]{3,2,1,0:T(8,128)}, f32[2,6,64,128]{3,2,1,0:T(8,128)}, f32[2,6,64,128]{3,2,1,0:T(8,1...) while((s32[]{:T(128)}, f32[6,128,128]{2,1,0:T(8,128)}, ...), condition=%wide.region_7.8_spmd, body=%wide.region_6.7_spmd.sunk | while | flops 264388608 | bytes 9046217 | solution.py:135
  150.5 2.6 %convolution_subtract_fusion.3 = f32[6,128,128]{2,1,0:T(8,128)} fusion(f32[6,128,128]{2,1,0:T(8,128)} %get-tuple-element.503, f32[6,64,128]{2,1,0:T(8,128)S(1)} %fusion.149, f32[2,6,64,128]{3,2,1,0:T(8,128)S(1)} %copy-done.4, s32[]{:T(128)} %get-tuple-element.502), kind=kOutput, calls=%fused_computation.25.clone.1 | convolution fusion | flops 75595776 | bytes 1179652 | tf_op jit(solution)/shard_map/while/body/eval_jaxpr/mjr,mjz->mrz/dot_general | solution.py:130
  157.4 2.6 %convolution_subtract_fusion.3 = f32[6,128,128]{2,1,0:T(8,128)} fusion(f32[6,128,128]{2,1,0:T(8,128)} %get-tuple-element.503, f32[6,64,128]{2,1,0:T(8,128)S(1)} %fusion.149, f32[2,6,64,128]{3,2,1,0:T(8,128)S(1)} %copy-done.4, s32[]{:T(128)} %get-tuple-element.502), kind=kOutput, calls=%fused_computation.25.clone.1 | convolution fusion | flops 75595776 | bytes 1179652 | tf_op jit(solution)/shard_map/while/body/eval_jaxpr/mjr,mjz->mrz/dot_general | solution.py:130
  160.0 1.9 %multiply_reduce_fusion = (f32[2,64,6]{1,2,0:T(8,128)S(1)}, f32[2,64,6,128]{3,1,2,0:T(8,128)}) fusion(f32[2,6,64,128]{3,2,1,0:T(8,128)} %get-tuple-element.179, f32[2,6,64,128]{3,2,1,0:T(8,128)} %get-tuple-element.182), kind=kLoop, calls=%fused_computation.77 | loop fusion | flops 294144 | bytes 1182720 | tf_op jit(solution)/shard_map/reduce_sum | solution.py:70
  162.8 1.9 %copy.63 = f32[128,768]{1,0:T(8,128)} copy(f32[128,768]{0,1:T(8,128)} %bitcast.156) | data formatting | bytes 786432 | tf_op jit(solution)/shard_map/mul | solution.py:71
  (101 shorter events, 51.2 us)
Async XLA Ops:
  6.5 12.3 %copy-start = (bf16[768,2304]{1,0:T(8,128)(2,1)S(1)}, bf16[768,2304]{1,0:T(8,128)(2,1)}, u32[]{:S(2)}) copy-start(bf16[768,2304]{1,0:T(8,128)(2,1)} %param.12) | copy-start | bytes 10616836
  8.3 10.5 %all-to-all-start = ((bf16[192,4,128]{2,0,1:T(8,128)(2,1)}), bf16[192,4,128]{2,0,1:T(8,128)(2,1)}, u32[]{:S(2)}, u32[]{:S(2)}) async-start(bf16[192,4,128]{2,0,1:T(8,128)(2,1)} %copy_bitcast_fusion), calls=%async_computation | async-start | bytes 393216 | tf_op jit(solution)/shard_map/all_to_all | solution.py:87
  13.5 88.9 %all-gather.5.cloned.1.call-start = ((), (), s32[]{:S(2)}) async-start(), calls=%async_computation.1 | async-start | bytes 1966080 | tf_op jit(solution)/shard_map/all_gather | solution.py:14
  35.2 2.1 %copy-start.11 = (pred[64,64]{1,0:T(8,128)(4,1)S(1)}, pred[64,64]{1,0:T(8,128)(4,1)}, u32[]{:S(2)}) copy-start(pred[64,64]{1,0:T(8,128)(4,1)} %iota_compare_fusion.2) | copy-start | bytes 12292
  37.3 1.9 %copy-start.1 = (f32[2,6,64,128]{3,2,1,0:T(8,128)}, f32[2,6,64,128]{3,2,1,0:T(8,128)S(1)}, u32[]{:S(2)}) copy-start(f32[2,6,64,128]{3,2,1,0:T(8,128)S(1)} %get-tuple-element.497) | copy-start | bytes 1179652
  37.3 1.9 %copy-start.10 = (f32[64,64]{1,0:T(8,128)S(1)}, f32[64,64]{1,0:T(8,128)}, u32[]{:S(2)}) copy-start(f32[64,64]{1,0:T(8,128)} %fusion.61) | copy-start | bytes 49156
  48.0 2.0 %copy-start.2 = (f32[2,6,64,128]{3,2,1,0:T(8,128)S(1)}, f32[2,6,64,128]{3,2,1,0:T(8,128)}, u32[]{:S(2)}) copy-start(f32[2,6,64,128]{3,2,1,0:T(8,128)} %copy-done.1) | copy-start | bytes 1179652
  52.3 2.9 %copy-start.5 = (f32[2,6,64,128]{3,2,1,0:T(8,128)S(1)}, f32[2,6,64,128]{3,2,1,0:T(8,128)}, u32[]{:S(2)}) copy-start(f32[2,6,64,128]{3,2,1,0:T(8,128)} %get-tuple-element.470) | copy-start | bytes 1179652 | tf_op jit(solution)/shard_map/while
  52.3 4.4 %copy-start.3 = (f32[2,6,64,128]{3,2,1,0:T(8,128)S(1)}, f32[2,6,64,128]{3,2,1,0:T(8,128)}, u32[]{:S(2)}) copy-start(f32[2,6,64,128]{3,2,1,0:T(8,128)} %get-tuple-element.467) | copy-start | bytes 1179652 | tf_op jit(solution)/shard_map/while
  55.1 4.4 %copy-start.6 = (f32[2,6,64,64]{3,2,1,0:T(8,128)S(1)}, f32[2,6,64,64]{3,2,1,0:T(8,128)}, u32[]{:S(2)}) copy-start(f32[2,6,64,64]{3,2,1,0:T(8,128)} %get-tuple-element.471) | copy-start | bytes 589828 | tf_op jit(solution)/shard_map/while
  60.6 2.9 %copy-start.5 = (f32[2,6,64,128]{3,2,1,0:T(8,128)S(1)}, f32[2,6,64,128]{3,2,1,0:T(8,128)}, u32[]{:S(2)}) copy-start(f32[2,6,64,128]{3,2,1,0:T(8,128)} %get-tuple-element.470) | copy-start | bytes 1179652 | tf_op jit(solution)/shard_map/while
  60.6 4.4 %copy-start.3 = (f32[2,6,64,128]{3,2,1,0:T(8,128)S(1)}, f32[2,6,64,128]{3,2,1,0:T(8,128)}, u32[]{:S(2)}) copy-start(f32[2,6,64,128]{3,2,1,0:T(8,128)} %get-tuple-element.467) | copy-start | bytes 1179652 | tf_op jit(solution)/shard_map/while
  63.4 4.4 %copy-start.6 = (f32[2,6,64,64]{3,2,1,0:T(8,128)S(1)}, f32[2,6,64,64]{3,2,1,0:T(8,128)}, u32[]{:S(2)}) copy-start(f32[2,6,64,64]{3,2,1,0:T(8,128)} %get-tuple-element.471) | copy-start | bytes 589828 | tf_op jit(solution)/shard_map/while
  71.0 64.1 %all-gather.7.cloned.1.call-start = ((), (), s32[]{:S(2)}) async-start(), calls=%async_computation.2 | async-start | bytes 1966080 | tf_op jit(solution)/shard_map/all_gather | solution.py:14
  146.1 3.2 %copy-start.7 = (f32[2,6,64,64]{3,2,1,0:T(8,128)S(1)}, f32[2,6,64,64]{3,2,1,0:T(8,128)}, u32[]{:S(2)}) copy-start(f32[2,6,64,64]{3,2,1,0:T(8,128)} %get-tuple-element.516) | copy-start | bytes 589828 | tf_op jit(solution)/shard_map/while
  146.1 3.3 %copy-start.8 = (f32[2,6,64,128]{3,2,1,0:T(8,128)S(1)}, f32[2,6,64,128]{3,2,1,0:T(8,128)}, u32[]{:S(2)}) copy-start(f32[2,6,64,128]{3,2,1,0:T(8,128)} %get-tuple-element.504) | copy-start | bytes 1179652 | tf_op jit(solution)/shard_map/while
  146.1 4.3 %copy-start.4 = (f32[2,6,64,128]{3,2,1,0:T(8,128)S(1)}, f32[2,6,64,128]{3,2,1,0:T(8,128)}, u32[]{:S(2)}) copy-start(f32[2,6,64,128]{3,2,1,0:T(8,128)} %get-tuple-element.513) | copy-start | bytes 1179652 | tf_op jit(solution)/shard_map/while
  149.7 0.8 copy-start.9
  153.0 3.2 %copy-start.7 = (f32[2,6,64,64]{3,2,1,0:T(8,128)S(1)}, f32[2,6,64,64]{3,2,1,0:T(8,128)}, u32[]{:S(2)}) copy-start(f32[2,6,64,64]{3,2,1,0:T(8,128)} %get-tuple-element.516) | copy-start | bytes 589828 | tf_op jit(solution)/shard_map/while
  153.0 3.3 %copy-start.8 = (f32[2,6,64,128]{3,2,1,0:T(8,128)S(1)}, f32[2,6,64,128]{3,2,1,0:T(8,128)}, u32[]{:S(2)}) copy-start(f32[2,6,64,128]{3,2,1,0:T(8,128)} %get-tuple-element.504) | copy-start | bytes 1179652 | tf_op jit(solution)/shard_map/while
  153.0 4.3 %copy-start.4 = (f32[2,6,64,128]{3,2,1,0:T(8,128)S(1)}, f32[2,6,64,128]{3,2,1,0:T(8,128)}, u32[]{:S(2)}) copy-start(f32[2,6,64,128]{3,2,1,0:T(8,128)} %get-tuple-element.513) | copy-start | bytes 1179652 | tf_op jit(solution)/shard_map/while
  156.6 0.8 copy-start.9
  160.0 6.0 %copy-start.12 = (f32[768]{0:T(1024)S(1)}, f32[768]{0:T(1024)}, u32[]{:S(2)}) copy-start(f32[768]{0:T(1024)} %param.15) | copy-start | bytes 9220
Sparse Core Ops, SparseCore 0:
  71.1 31.2 all-gather.4
  104.3 30.8 all-gather.6
where the time goes:
time: 176 us; the launch traced here: 175 us
  waiting for transfers between devices  65.4 us (37%)
  matrix products  46.7 us (27%)
  local copies, waits for them, and re-layouts  30.2 us (17%)
  between operations  13.6 us (8%)
  other arithmetic  13 us (7%)
  starting transfers between devices  5.42 us (3%)
    all_gather x2, waiting for transfers between devices, entering(): pieces = jax.tree.map(lambda part: lax.all_gather(part, axis), value)  63.4 us
    dot_general x3, matrix products, compose(): jnp.einsum('hij,hjk->hik', second_move, first_offset, precision=HIGHEST_A...  7.21 us
    dot_general x2, matrix products, first_pass(): jnp.einsum('mjr,mjz->mrz', key_block, target_value, precision=HIGHEST_ACC...  5.78 us
    all_to_all x1, starting transfers between devices, body(): lax.all_to_all(feats, 'seq', split_axis=1, concat_axis=0, tiled=True)  5.19 us
    dot_general x2, matrix products, second_pass(): jnp.einsum('mjr,mjz->mrz', key_block, held_value, precision=HIGHEST_ACCUR...  5.12 us
    while x31, local copies, waits for them, and re-layouts  4.53 us
    dot_general x2, matrix products, first_pass(): jnp.einsum('rnf,rfw->rnw', weight_block, joint_matrix, precision=HIGHEST_...  3.72 us
  transfers between devices with their start and end apart: 3, of which 3 were waited for; matrix products, arithmetic and copies ran while one was open for 2% of the time, Pallas kernels for 0%

commit v1 on v0

--- a/solution.py
+++ b/solution.py
@@ -7,6 +7,28 @@
 HD = 128
 GROUP = 64
 HIGHEST_ACCURACY = lax.Precision.HIGHEST
+
+
+def cut_along(x, dim, size):
+    before, after = (x.shape[:dim], x.shape[dim + 1 :])
+    return jnp.moveaxis(x.reshape(*before, size, -1, *after), dim, 0)
+
+
+def in_order(tiles, dim):
+    tiles = jnp.moveaxis(tiles, 0, dim)
+    lengths = tiles.shape
+    return tiles.reshape(*lengths[:dim], lengths[dim] * lengths[dim + 1], *lengths[dim + 2 :])
+
+
+def swapped_with_each(x, axis, split_dim, concat_dim):
+    size, index = (lax.axis_size(axis), lax.axis_index(axis))
+    blocks = cut_along(x, split_dim, size)
+    outs = [blocks[index]]
+    for step in range(1, size):
+        sent = blocks[index ^ step]
+        outs.append(lax.ppermute(sent, axis, [(i, i ^ step) for i in range(size)]))
+    blocks = jnp.stack(outs)[index ^ jnp.arange(size)]
+    return in_order(blocks, concat_dim)
 
 
 def entering(value, axis, join, neutral):
@@ -84,7 +106,7 @@
 
 
 def body(feats, qkv_weight, beta_weight, beta_bias, out_gain):
-    local = lax.all_to_all(feats, "seq", split_axis=1, concat_axis=0, tiled=True)
+    local = swapped_with_each(feats, "seq", 1, 0)
     qkv = lax.dot_general(
         local, qkv_weight, (((0,), (0,)), ((), ())), preferred_element_type=jnp.float32
     ).astype(jnp.bfloat16)

time: 176 us -> 183 us (1.040)
  local copies, waits for them, and re-layouts: 30.2 us -> 38.1 us
    all_to_all x1 -> x0, starting transfers between devices: 5.19 us -> none  [body(): lax.all_to_all(feats, 'seq', split_axis=1, concat_axis=0, tiled=True)]
    ppermute x0 -> x3, starting transfers between devices: none -> 4.49 us  [swapped_with_each(): outs.append(lax.ppermute(sent, axis, [(i, i ^ step) for i in range(size)]))]
    unnamed x12 -> x20, local copies, waits for them, and re-layouts: 0.02 us -> 2.8 us
    another operation x2 -> x3, local copies, waits for them, and re-layouts: 1.58 us -> 3.88 us
    gather x0 -> x1, local copies, waits for them, and re-layouts: none -> 2.16 us  [swapped_with_each(): blocks = jnp.stack(outs)[index ^ jnp.arange(size)]]
  transfers between devices with their start and end apart: 3 -> 5, of which waited for: 3 -> 3; matrix products, arithmetic and copies ran while one was open for 2% -> 3% of each run, Pallas kernels for 0% -> 0%
where the time goes in v1:
time: 183 us; the launch traced here: 182 us
  waiting for transfers between devices  65.4 us (36%)
  matrix products  46.6 us (25%)
  local copies, waits for them, and re-layouts  38.1 us (21%)
  between operations  13.6 us (7%)
  other arithmetic  13.5 us (7%)
  starting transfers between devices  4.53 us (2%)
    all_gather x2, waiting for transfers between devices, entering(): pieces = jax.tree.map(lambda part: lax.all_gather(part, axis), value)  64.1 us
    dot_general x3, matrix products, compose(): jnp.einsum('hij,hjk->hik', second_move, first_offset, precision=HIGHEST_A...  7.19 us
    dot_general x2, matrix products, first_pass(): jnp.einsum('mjr,mjz->mrz', key_block, target_value, precision=HIGHEST_ACC...  5.77 us
    dot_general x2, matrix products, second_pass(): jnp.einsum('mjr,mjz->mrz', key_block, held_value, precision=HIGHEST_ACCUR...  5.11 us
    while x31, local copies, waits for them, and re-layouts  4.52 us
    ppermute x3, starting transfers between devices, swapped_with_each(): outs.append(lax.ppermute(sent, axis, [(i, i ^ step) for i in range(size)]))  4.49 us
    another operation x3, local copies, waits for them, and re-layouts  3.88 us
    dot_general x2, matrix products, first_pass(): jnp.einsum('rnf,rfw->rnw', weight_block, joint_matrix, precision=HIGHEST_...  3.72 us
  transfers between devices with their start and end apart: 5, of which 3 were waited for; matrix products, arithmetic and copies ran while one was open for 3% of the time, Pallas kernels for 0%

profile of v1, /device:TPU:0, one launch (start us, length us, event | category | flops | bytes accessed | tf_op | source)
XLA Modules:
  0.0 181.8 jit_solution(7164224820717150084)
XLA Ops:
  8.3 2.3 %constant_dynamic-slice_fusion.3 = (bf16[192,1,128]{2,1,0:T(2,128)(2,1)}, bf16[192,1,128]{2,1,0:T(2,128)(2,1)S(1)}, bf16[192,1,128]{2,1,0:T(2,128)(2,1)S(1)}, bf16[192,1,128]{2,1,0:T(2,128)(2,1)S(1)}) fusion(bf16[192,4,128]{2,1,0:T(4,128)(2,1)} %reshape.102, s32[]{:T(128)S(6)} %select_n.52, s32[]{:T(128)S(6)} %select_n.55, s32[]{:T(128)S(6)} %select_n.54, ...), kind=kLoop, calls=%fused_computation.105 | loop fusion | bytes 393232 | tf_op jit(solution)/shard_map/dynamic-slice
  11.3 3.0 %collective-permute-start = (bf16[192,128]{1,0:T(8,128)(2,1)}, bf16[192,128]{1,0:T(8,128)(2,1)}, u32[]{:S(2)}, u32[]{:S(2)}) collective-permute-start(bf16[192,128]{1,0:T(8,128)(2,1)} %bitcast.123), channel_id=1, source_target_pairs={{0,8},{8,0},{16,24},{24,16},{1,9},{9,1},{17,25},{25,17},{2,10},{10... | collective-permute-start | bytes 147464 | tf_op jit(solution)/shard_map/ppermute | solution.py:29
  23.8 2.2 %gather_fusion = bf16[4,192,128]{2,1,0:T(8,128)(2,1)} fusion(bf16[4,192,128]{2,1,0:T(8,128)(2,1)} %pad_maximum_fusion, s32[1024]{0:T(1024)S(1)} %pad_clamp_fusion), kind=kCustom, calls=%fused_computation | custom fusion | bytes 393232 | tf_op jit(solution)/shard_map/gather | solution.py:30
  26.0 2.6 %fusion.45 = f32[128,2304]{1,0:T(8,128)} fusion(bf16[768,128]{1,0:T(8,128)(2,1)} %bitcast.169, bf16[768,2304]{1,0:T(8,128)(2,1)S(1)} %copy-done), kind=kOutput, calls=%fused_computation.54 | convolution fusion | flops 453574656 | bytes 4915200 | tf_op jit(solution)/shard_map/dot_general | solution.py:110
  28.6 2.7 %copy.47 = f32[128,2304]{0,1:T(8,128)} copy(f32[128,2304]{1,0:T(8,128)} %fusion.45) | data formatting | bytes 2359296 | tf_op jit(solution)/shard_map/reshape | solution.py:64
  31.3 2.3 %multiply_reduce_fusion.1 = (f32[128,6]{0,1:T(8,128)S(1)}, f32[128,6]{0,1:T(8,128)S(1)}, f32[128,1,6,128]{0,3,2,1:T(8,128)}, f32[128,1,6,128]{0,3,2,1:T(8,128)}, f32[128,1,6,128]{0,3,2,1:T(8,128)}) fusion(f32[128,3,6,128]{0,3,2,1:T(8,128)} %bitcast.161), kind=kLoop, calls=%fused_computation.81 | loop fusion | flops 391680 | bytes 2365440 | tf_op jit(solution)/shard_map/reduce_sum | solution.py:68
  33.6 1.9 %copy.54 = f32[128,1,6,128]{3,0,2,1:T(8,128)} copy(f32[128,1,6,128]{0,3,2,1:T(8,128)} %get-tuple-element.309) | data formatting | bytes 786432 | tf_op jit(solution)/shard_map/slice | solution.py:65
  37.5 1.9 %copy.48 = f32[128,1,6,128]{3,0,2,1:T(8,128)} copy(f32[128,1,6,128]{0,3,2,1:T(8,128)} %get-tuple-element.311) | data formatting | bytes 786432 | tf_op jit(solution)/shard_map/slice | solution.py:66
  39.4 1.9 %copy.52 = f32[128,1,6,128]{3,0,2,1:T(8,128)} copy(f32[128,1,6,128]{0,3,2,1:T(8,128)} %get-tuple-element.310) | data formatting | bytes 786432 | tf_op jit(solution)/shard_map/slice | solution.py:67
  58.9 16.6 %while.38 = (s32[]{:T(128)}, f32[6,128,256]{2,1,0:T(8,128)}, f32[2,6,64,128]{3,2,1,0:T(8,128)}, f32[2,6,64,128]{3,2,1,0:T(8,128)}, f32[2,6,64,128]{3,2,1,0:T(8,1...) while((s32[]{:T(128)}, f32[6,128,256]{2,1,0:T(8,128)}, ...), condition=%wide.region_3.4_spmd, body=%wide.region_2.3_spmd.sunk | while | flops 415678464 | bytes 10029241 | solution.py:138
  63.4 2.9 %convolution_add_fusion.10 = f32[6,128,256]{2,1,0:T(8,128)} fusion(f32[6,128,256]{2,1,0:T(8,128)} %get-tuple-element.460, f32[6,64,128]{2,1,0:T(8,128)S(1)} %get-tuple-element.436, f32[6,64,128]{2,1,0:T(8,128)S(1)} %get-tuple-element.437, f32[2,6,64,128]{3,2,1,0:T(8,128)S(1)} %copy-done.2, s32[]{:T(128)} %get-tuple-element.459), kind=kOutput, calls=%fused_computation.1.clone.1 | convolution fusion | flops 151289856 | bytes 2162692 | tf_op jit(solution)/shard_map/while/body/eval_jaxpr/mjr,mjz->mrz/dot_general | solution.py:132
  71.7 2.9 %convolution_add_fusion.10 = f32[6,128,256]{2,1,0:T(8,128)} fusion(f32[6,128,256]{2,1,0:T(8,128)} %get-tuple-element.460, f32[6,64,128]{2,1,0:T(8,128)S(1)} %get-tuple-element.436, f32[6,64,128]{2,1,0:T(8,128)S(1)} %get-tuple-element.437, f32[2,6,64,128]{3,2,1,0:T(8,128)S(1)} %copy-done.2, s32[]{:T(128)} %get-tuple-element.459), kind=kOutput, calls=%fused_computation.1.clone.1 | convolution fusion | flops 151289856 | bytes 2162692 | tf_op jit(solution)/shard_map/while/body/eval_jaxpr/mjr,mjz->mrz/dot_general | solution.py:132
  75.5 2.1 %fusion.66 = (f32[6,128,128]{2,1,0:T(8,128)}, f32[6,128,128]{2,1,0:T(8,128)}) fusion(f32[6,128,256]{2,1,0:T(8,128)} %get-tuple-element.180), kind=kLoop, calls=%fused_computation.110 | loop fusion | bytes 1572864 | tf_op jit(solution)/shard_map/slice | solution.py:140
  78.4 31.4 %all-gather.5.cloned.1.call-done = f32[24,128,128]{2,1,0:T(8,128)} async-done(((f32[6,128,128]{2,1,0:T(8,128)}), f32[24,128,128]{2,1,0:T(8,128)}) %all-gather.5.cloned.1.call-update) | async-done | bytes 1572880 | tf_op jit(solution)/shard_map/all_gather | solution.py:36
  109.8 32.7 %all-gather.7.cloned.1.call-done = f32[24,128,128]{2,1,0:T(8,128)} async-done(((f32[6,128,128]{2,1,0:T(8,128)}), f32[24,128,128]{2,1,0:T(8,128)}) %all-gather.7.cloned.1.call-update) | async-done | bytes 1572880 | tf_op jit(solution)/shard_map/all_gather | solution.py:36
  142.5 10.2 %while.40 = (s32[]{:T(128)}, f32[6,128,128]{2,1,0:T(8,128)}, s32[]{:T(128)}, f32[4,6,128,128]{3,2,1,0:T(8,128)}, f32[4,6,128,128]{3,2,1,0:T(8,128)}, /*index=5*/s32[]{:T(128)}, s32[]{:T(128)}) while((s32[]{:T(128)}, f32[6,128,128]{2,1,0:T(8,128)}, s32[]{:T(128)}, f32[4,6,128,128]{3,2,1,0:T(8,128)}, f32[4,6,128,128]{3,2,1,0:T(8,128)}, ...), condition=%wide.region_5.6_spmd.clone, body=%wide.region_4.5_spmd.clone.sunk | while | flops 151388160 | bytes 2755167 | solution.py:45
  143.5 2.4 %fusion.154 = f32[6,128,128]{2,1,0:T(8,128)} fusion(f32[6,128,128]{2,1,0:T(8,128)S(1)} %copy.112, f32[4,6,128,128]{3,2,1,0:T(8,128)} %get-tuple-element.495, s32[]{:T(128)} %get-tuple-element.484, f32[4,6,128,128]{3,2,1,0:T(8,128)} %get-tuple-element.494, pred[]{:T(512)S(6)} %compare.4, pred[]{:T(512)S(6)} %lt.60), kind=kOutput, calls=%fused_computation.45.clone.1 | convolution fusion | flops 151388160 | bytes 1968640 | tf_op jit(solution)/shard_map/while/body/eval_jaxpr/hij,hjk->hik/dot_general | solution.py:102
  146.9 2.4 %fusion.154 = f32[6,128,128]{2,1,0:T(8,128)} fusion(f32[6,128,128]{2,1,0:T(8,128)S(1)} %copy.112, f32[4,6,128,128]{3,2,1,0:T(8,128)} %get-tuple-element.495, s32[]{:T(128)} %get-tuple-element.484, f32[4,6,128,128]{3,2,1,0:T(8,128)} %get-tuple-element.494, pred[]{:T(512)S(6)} %compare.4, pred[]{:T(512)S(6)} %lt.60), kind=kOutput, calls=%fused_computation.45.clone.1 | convolution fusion | flops 151388160 | bytes 1968640 | tf_op jit(solution)/shard_map/while/body/eval_jaxpr/hij,hjk->hik/dot_general | solution.py:102
  150.3 2.4 %fusion.154 = f32[6,128,128]{2,1,0:T(8,128)} fusion(f32[6,128,128]{2,1,0:T(8,128)S(1)} %copy.112, f32[4,6,128,128]{3,2,1,0:T(8,128)} %get-tuple-element.495, s32[]{:T(128)} %get-tuple-element.484, f32[4,6,128,128]{3,2,1,0:T(8,128)} %get-tuple-element.494, pred[]{:T(512)S(6)} %compare.4, pred[]{:T(512)S(6)} %lt.60), kind=kOutput, calls=%fused_computation.45.clone.1 | convolution fusion | flops 151388160 | bytes 1968640 | tf_op jit(solution)/shard_map/while/body/eval_jaxpr/hij,hjk->hik/dot_general | solution.py:102
  153.5 13.8 %while.39 = (s32[]{:T(128)}, f32[6,128,128]{2,1,0:T(8,128)}, f32[2,6,64,128]{3,2,1,0:T(8,128)}, f32[2,6,64,128]{3,2,1,0:T(8,128)}, f32[2,6,64,128]{3,2,1,0:T(8,1...) while((s32[]{:T(128)}, f32[6,128,128]{2,1,0:T(8,128)}, ...), condition=%wide.region_7.8_spmd, body=%wide.region_6.7_spmd.sunk | while | flops 264388608 | bytes 9046217 | solution.py:157
  157.8 2.6 %convolution_subtract_fusion.3 = f32[6,128,128]{2,1,0:T(8,128)} fusion(f32[6,128,128]{2,1,0:T(8,128)} %get-tuple-element.507, f32[6,64,128]{2,1,0:T(8,128)S(1)} %fusion.149, f32[2,6,64,128]{3,2,1,0:T(8,128)S(1)} %copy-done.3, s32[]{:T(128)} %get-tuple-element.506), kind=kOutput, calls=%fused_computation.26.clone.1 | convolution fusion | flops 75595776 | bytes 1179652 | tf_op jit(solution)/shard_map/while/body/eval_jaxpr/mjr,mjz->mrz/dot_general | solution.py:152
  164.7 2.6 %convolution_subtract_fusion.3 = f32[6,128,128]{2,1,0:T(8,128)} fusion(f32[6,128,128]{2,1,0:T(8,128)} %get-tuple-element.507, f32[6,64,128]{2,1,0:T(8,128)S(1)} %fusion.149, f32[2,6,64,128]{3,2,1,0:T(8,128)S(1)} %copy-done.3, s32[]{:T(128)} %get-tuple-element.506), kind=kOutput, calls=%fused_computation.26.clone.1 | convolution fusion | flops 75595776 | bytes 1179652 | tf_op jit(solution)/shard_map/while/body/eval_jaxpr/mjr,mjz->mrz/dot_general | solution.py:152
  167.3 1.9 %multiply_reduce_fusion = (f32[2,64,6]{1,2,0:T(8,128)S(1)}, f32[2,64,6,128]{3,1,2,0:T(8,128)}) fusion(f32[2,6,64,128]{3,2,1,0:T(8,128)} %get-tuple-element.179, f32[2,6,64,128]{3,2,1,0:T(8,128)} %get-tuple-element.182), kind=kLoop, calls=%fused_computation.78 | loop fusion | flops 294144 | bytes 1182720 | tf_op jit(solution)/shard_map/reduce_sum | solution.py:92
  170.1 1.9 %copy.60 = f32[128,768]{1,0:T(8,128)} copy(f32[128,768]{0,1:T(8,128)} %bitcast.166) | data formatting | bytes 786432 | tf_op jit(solution)/shard_map/mul | solution.py:93
  (118 shorter events, 59.2 us)
Async XLA Ops:
  6.5 19.5 %copy-start = (bf16[768,2304]{1,0:T(8,128)(2,1)S(1)}, bf16[768,2304]{1,0:T(8,128)(2,1)}, u32[]{:S(2)}) copy-start(bf16[768,2304]{1,0:T(8,128)(2,1)} %param.12) | copy-start | bytes 10616836
  6.5 103.2 %all-gather.5.cloned.1.call-start = ((), (), s32[]{:S(2)}) async-start(), calls=%async_computation | async-start | bytes 1966080 | tf_op jit(solution)/shard_map/all_gather | solution.py:36
  11.3 10.4 %collective-permute-start = (bf16[192,128]{1,0:T(8,128)(2,1)}, bf16[192,128]{1,0:T(8,128)(2,1)}, u32[]{:S(2)}, u32[]{:S(2)}) collective-permute-start(bf16[192,128]{1,0:T(8,128)(2,1)} %bitcast.123), channel_id=1, source_target_pairs={{0,8},{8,0},{16,24},{24,16},{1,9},{9,1},{17,25},{25,17},{2,10},{10... | collective-permute-start | bytes 147464 | tf_op jit(solution)/shard_map/ppermute | solution.py:29
  14.8 6.8 %collective-permute-start.1 = (bf16[192,128]{1,0:T(8,128)(2,1)}, bf16[192,128]{1,0:T(8,128)(2,1)}, u32[]{:S(2)}, u32[]{:S(2)}) collective-permute-start(bf16[192,128]{1,0:T(8,128)(2,1)} %bitcast.122), channel_id=1, source_target_pairs={{0,16},{8,24},{16,0},{24,8},{1,17},{9,25},{17,1},{25,9},{2,18},{10... | collective-permute-start | bytes 147464 | tf_op jit(solution)/shard_map/ppermute | solution.py:29
  17.0 5.3 %collective-permute-start.2 = (bf16[192,128]{1,0:T(8,128)(2,1)}, bf16[192,128]{1,0:T(8,128)(2,1)}, u32[]{:S(2)}, u32[]{:S(2)}) collective-permute-start(bf16[192,128]{1,0:T(8,128)(2,1)} %bitcast.121), channel_id=1, source_target_pairs={{0,24},{8,16},{16,8},{24,0},{1,25},{9,17},{17,9},{25,1},{2,26},{10... | collective-permute-start | bytes 147464 | tf_op jit(solution)/shard_map/ppermute | solution.py:29
  36.1 5.2 %copy-start.13 = (f32[128,6]{0,1:T(8,128)S(1)}, f32[128,6]{0,1:T(8,128)}, u32[]{:S(2)}) copy-start(f32[128,6]{0,1:T(8,128)} %get-tuple-element.322) | copy-start | bytes 9220
  45.7 2.7 %copy-start.9 = (f32[128,1,6,128]{3,0,2,1:T(8,128)S(1)}, f32[128,1,6,128]{3,0,2,1:T(8,128)}, u32[]{:S(2)}) copy-start(f32[128,1,6,128]{3,0,2,1:T(8,128)} %copy.48) | copy-start | bytes 1179652
  45.7 2.7 %copy-start.10 = (f32[128,1,6,128]{3,0,2,1:T(8,128)S(1)}, f32[128,1,6,128]{3,0,2,1:T(8,128)}, u32[]{:S(2)}) copy-start(f32[128,1,6,128]{3,0,2,1:T(8,128)} %copy.52) | copy-start | bytes 1179652
  48.7 2.8 %copy-start.1 = (f32[2,6,64,128]{3,2,1,0:T(8,128)}, f32[2,6,64,128]{3,2,1,0:T(8,128)S(1)}, u32[]{:S(2)}) copy-start(f32[2,6,64,128]{3,2,1,0:T(8,128)S(1)} %get-tuple-element.501) | copy-start | bytes 1179652
  50.2 1.9 %copy-start.11 = (f32[64,64]{1,0:T(8,128)S(1)}, f32[64,64]{1,0:T(8,128)}, u32[]{:S(2)}) copy-start(f32[64,64]{1,0:T(8,128)} %fusion.61) | copy-start | bytes 49156
  58.9 2.9 %copy-start.4 = (f32[2,6,64,128]{3,2,1,0:T(8,128)S(1)}, f32[2,6,64,128]{3,2,1,0:T(8,128)}, u32[]{:S(2)}) copy-start(f32[2,6,64,128]{3,2,1,0:T(8,128)} %get-tuple-element.474) | copy-start | bytes 1179652 | tf_op jit(solution)/shard_map/while
  58.9 4.4 %copy-start.2 = (f32[2,6,64,128]{3,2,1,0:T(8,128)S(1)}, f32[2,6,64,128]{3,2,1,0:T(8,128)}, u32[]{:S(2)}) copy-start(f32[2,6,64,128]{3,2,1,0:T(8,128)} %get-tuple-element.471) | copy-start | bytes 1179652 | tf_op jit(solution)/shard_map/while
  61.8 4.4 %copy-start.5 = (f32[2,6,64,64]{3,2,1,0:T(8,128)S(1)}, f32[2,6,64,64]{3,2,1,0:T(8,128)}, u32[]{:S(2)}) copy-start(f32[2,6,64,64]{3,2,1,0:T(8,128)} %get-tuple-element.475) | copy-start | bytes 589828 | tf_op jit(solution)/shard_map/while
  67.2 2.9 %copy-start.4 = (f32[2,6,64,128]{3,2,1,0:T(8,128)S(1)}, f32[2,6,64,128]{3,2,1,0:T(8,128)}, u32[]{:S(2)}) copy-start(f32[2,6,64,128]{3,2,1,0:T(8,128)} %get-tuple-element.474) | copy-start | bytes 1179652 | tf_op jit(solution)/shard_map/while
  67.2 4.4 %copy-start.2 = (f32[2,6,64,128]{3,2,1,0:T(8,128)S(1)}, f32[2,6,64,128]{3,2,1,0:T(8,128)}, u32[]{:S(2)}) copy-start(f32[2,6,64,128]{3,2,1,0:T(8,128)} %get-tuple-element.471) | copy-start | bytes 1179652 | tf_op jit(solution)/shard_map/while
  70.1 4.4 %copy-start.5 = (f32[2,6,64,64]{3,2,1,0:T(8,128)S(1)}, f32[2,6,64,64]{3,2,1,0:T(8,128)}, u32[]{:S(2)}) copy-start(f32[2,6,64,64]{3,2,1,0:T(8,128)} %get-tuple-element.475) | copy-start | bytes 589828 | tf_op jit(solution)/shard_map/while
  77.7 64.8 %all-gather.7.cloned.1.call-start = ((), (), s32[]{:S(2)}) async-start(), calls=%async_computation.1 | async-start | bytes 1966080 | tf_op jit(solution)/shard_map/all_gather | solution.py:36
  153.5 3.2 %copy-start.6 = (f32[2,6,64,64]{3,2,1,0:T(8,128)S(1)}, f32[2,6,64,64]{3,2,1,0:T(8,128)}, u32[]{:S(2)}) copy-start(f32[2,6,64,64]{3,2,1,0:T(8,128)} %get-tuple-element.520) | copy-start | bytes 589828 | tf_op jit(solution)/shard_map/while
  153.5 3.3 %copy-start.7 = (f32[2,6,64,128]{3,2,1,0:T(8,128)S(1)}, f32[2,6,64,128]{3,2,1,0:T(8,128)}, u32[]{:S(2)}) copy-start(f32[2,6,64,128]{3,2,1,0:T(8,128)} %get-tuple-element.508) | copy-start | bytes 1179652 | tf_op jit(solution)/shard_map/while
  153.5 4.3 %copy-start.3 = (f32[2,6,64,128]{3,2,1,0:T(8,128)S(1)}, f32[2,6,64,128]{3,2,1,0:T(8,128)}, u32[]{:S(2)}) copy-start(f32[2,6,64,128]{3,2,1,0:T(8,128)} %get-tuple-element.517) | copy-start | bytes 1179652 | tf_op jit(solution)/shard_map/while
  160.4 3.2 %copy-start.6 = (f32[2,6,64,64]{3,2,1,0:T(8,128)S(1)}, f32[2,6,64,64]{3,2,1,0:T(8,128)}, u32[]{:S(2)}) copy-start(f32[2,6,64,64]{3,2,1,0:T(8,128)} %get-tuple-element.520) | copy-start | bytes 589828 | tf_op jit(solution)/shard_map/while
  160.4 3.3 %copy-start.7 = (f32[2,6,64,128]{3,2,1,0:T(8,128)S(1)}, f32[2,6,64,128]{3,2,1,0:T(8,128)}, u32[]{:S(2)}) copy-start(f32[2,6,64,128]{3,2,1,0:T(8,128)} %get-tuple-element.508) | copy-start | bytes 1179652 | tf_op jit(solution)/shard_map/while
  160.4 4.3 %copy-start.3 = (f32[2,6,64,128]{3,2,1,0:T(8,128)S(1)}, f32[2,6,64,128]{3,2,1,0:T(8,128)}, u32[]{:S(2)}) copy-start(f32[2,6,64,128]{3,2,1,0:T(8,128)} %get-tuple-element.517) | copy-start | bytes 1179652 | tf_op jit(solution)/shard_map/while
  167.3 6.0 %copy-start.14 = (f32[768]{0:T(1024)S(1)}, f32[768]{0:T(1024)}, u32[]{:S(2)}) copy-start(f32[768]{0:T(1024)} %param.15) | copy-start | bytes 9220
  (3 other events, 3.3 us)
Sparse Core Ops, SparseCore 0:
  77.8 31.9 all-gather.4
  111.6 30.8 all-gather.6
